TPU v7x, 32 devices: a whole 2x2x4 slice. The times are simulated.
32 devices in a mesh: groups: 2 (over y), chan: 4 (over z), tm: 4 (over x, core).
Axes of the slice: x: 2, y: 2, z: 4, core: 2. Of those that a mesh axis runs over, the one named last changes fastest.
Arguments:
- samples: bfloat16 [2, 16, 1024, 4096], P(None, None, ('groups', 'chan'), 'tm'), parts along dimension 2, may hold values from -6 to 6
- station_gain: float32 [1024], P(('groups', 'chan')), parts along dimension 0, may hold values from 0.5 to 4
- station_map: int32 [1024], P('groups'), parts along dimension 0, may hold values from 0 to 511, each once
- steer_phase: float32 [16, 512, 1024], P('chan', None, ('groups', 'tm')), parts along dimension 2, may hold values from -3.140625 to 3.140625
Outputs:
- beams_out: bfloat16 [16, 4096, 2, 1024], P('chan', 'tm', None, 'groups'), parts along dimension 3
There are 2 independent parts, one for each index of `groups`. A program takes and returns all parts, laid end to end along the dimension named above; each array names one. Nothing has to cross between parts.
Inputs may be any that keep to these rules, and one draw needn't show every extreme that they name: station_map names each of the 512 stations once.
All inputs are finite; a program needn't handle non-finite values.
Results may differ from a plain program's by a relative error of at most 0.015.
Values may be sent and summed in bfloat16 or wider, within the bound.
No kernel may reach another device: no remote copies, remote signals or barrier semaphores. Data moves between devices by JAX's collectives and lax.ppermute only.
A program may use at most 256 MiB of HBM per device.

v0:
```python
import math
import jax
import jax.numpy as jnp
from jax import lax
from jax.sharding import PartitionSpec as P

ITERS = 8


def dft_table(count):
    index = jnp.arange(count, dtype=jnp.int32)
    turns = (index[:, None] * index[None, :] % count).astype(jnp.float32)
    angle_grid = 2.0 * math.pi * turns / count
    cosine = jnp.cos(angle_grid)
    sine = jnp.sin(angle_grid)
    upper = jnp.concatenate((cosine, sine), axis=1)
    lower = jnp.concatenate((-sine, cosine), axis=1)
    return jnp.concatenate((upper, lower), axis=0).astype(jnp.bfloat16)


def gram_blocks(stacked):
    return jnp.einsum("cat,cbt->cab", stacked, stacked, preferred_element_type=jnp.float32)


def local(samples, station_gain, station_map, steer_phase):
    high = lax.Precision.HIGHEST
    count = samples.shape[1]
    row_count = samples.shape[2]
    spec_count = samples.shape[3]
    channelized = jnp.dot(
        dft_table(count), samples.reshape(2 * count, -1), preferred_element_type=jnp.float32
    )
    channelized = channelized.reshape(2, count, row_count, spec_count)
    spectra = (channelized * station_gain[None, None, :, None]).astype(jnp.bfloat16)
    owned = lax.all_to_all(spectra, "chan", split_axis=1, concat_axis=2, tiled=True)
    stations = owned.shape[2]
    stacked = jnp.concatenate((owned[0], owned[1]), axis=1)
    spectra_total = spec_count * lax.axis_size("tm")
    gram_sum = gram_blocks(stacked)
    part_real = gram_sum[:, :stations, :stations] + gram_sum[:, stations:, stations:]
    part_imag = gram_sum[:, stations:, :stations] - gram_sum[:, :stations, stations:]
    cov_real, cov_imag = (
        lax.psum(part_real.astype(jnp.bfloat16), "tm").astype(jnp.float32),
        lax.psum(part_imag.astype(jnp.bfloat16), "tm").astype(jnp.float32),
    )
    cov_real = cov_real / spectra_total
    cov_imag = cov_imag / spectra_total
    loading = jnp.sum(jnp.diagonal(cov_real, axis1=1, axis2=2), axis=1) / stations
    row_mass = jnp.sum(jnp.sqrt(cov_real * cov_real + cov_imag * cov_imag), axis=2)
    bound = loading + jnp.max(row_mass, axis=1)
    center = ((bound + loading) / 2.0)[:, None, None]
    radius = ((bound - loading) / 2.0)[:, None, None]
    loading = loading[:, None, None]
    phase_rows = jnp.take(steer_phase, station_map, axis=1)
    steer_real = jnp.cos(phase_rows)
    steer_imag = jnp.sin(phase_rows)
    sol_real = jnp.zeros_like(steer_real)
    sol_imag = jnp.zeros_like(steer_imag)
    res_real, res_imag = (steer_real, steer_imag)
    dir_real = res_real / center
    dir_imag = res_imag / center
    rho_prev = radius / center
    for iteration in range(ITERS):
        sol_real = sol_real + dir_real
        sol_imag = sol_imag + dir_imag
        out_real = jnp.einsum("cjk,ckb->cjb", cov_real, dir_real, precision=high) - jnp.einsum(
            "cjk,ckb->cjb", cov_imag, dir_imag, precision=high
        )
        out_imag = jnp.einsum("cjk,ckb->cjb", cov_imag, dir_real, precision=high) + jnp.einsum(
            "cjk,ckb->cjb", cov_real, dir_imag, precision=high
        )
        img_real = out_real + loading * dir_real
        img_imag = out_imag + loading * dir_imag
        res_real = res_real - img_real
        res_imag = res_imag - img_imag
        rho_next = 1.0 / (2.0 * center / radius - rho_prev)
        dir_real = rho_next * rho_prev * dir_real + 2.0 * rho_next / radius * res_real
        dir_imag = rho_next * rho_prev * dir_imag + 2.0 * rho_next / radius * res_imag
        rho_prev = rho_next
    response = jnp.sum(steer_real * sol_real + steer_imag * sol_imag, axis=1, keepdims=True)
    weights = jnp.stack(
        ((sol_real / response).astype(jnp.bfloat16), (sol_imag / response).astype(jnp.bfloat16)),
        axis=1,
    )
    block_part = lax.all_gather(weights, "tm", axis=3, tiled=True)
    weight_real = block_part[:, 0]
    weight_imag = block_part[:, 1]
    weight_cat = jnp.stack(
        (
            jnp.concatenate((weight_real, weight_imag), axis=1),
            jnp.concatenate((-weight_imag, weight_real), axis=1),
        ),
        axis=2,
    )
    formed = jnp.einsum("cat,cakb->ctkb", stacked, weight_cat, preferred_element_type=jnp.float32)
    return formed.astype(jnp.bfloat16)


def solution(mesh):
    in_specs = (
        P(None, None, ("groups", "chan"), "tm"),
        P(("groups", "chan")),
        P("groups"),
        P("chan", None, ("groups", "tm")),
    )
    out_specs = P("chan", "tm", None, "groups")
    return jax.shard_map(local, mesh=mesh, in_specs=in_specs, out_specs=out_specs, check_vma=False)
```

profile of v0, /device:TPU:0, one launch (start us, length us, event | category | flops | bytes accessed | tf_op | source)
XLA Modules:
  0.0 677.3 jit_solution(14381816873697495504)
XLA Ops:
  6.7 17.6 %multiply_convert_fusion = bf16[2,16,128,1024]{3,1,2,0:T(8,128)(2,1)} fusion(f32[128]{0:T(128)} %param.5, bf16[2,16,32,1]{2,1,3,0:T(8,128)(2,1)S(1)} %bitcast.120, bf16[4,8,128,1024]{3,2,1,0:T(8,128)(2,1)} %bitcast.121), kind=kOutput, calls=%fused_computation.2 | convolution fusion | flops 276824064 | bytes 16779776 | tf_op jit(solution)/shard_map/dot_general | solution.py:30
  24.4 11.3 %copy.26 = bf16[2,16,128,1024]{3,2,0,1:T(8,128)(2,1)} copy(bf16[2,16,128,1024]{3,1,2,0:T(8,128)(2,1)} %multiply_convert_fusion) | data formatting | bytes 16777216 | tf_op jit(solution)/shard_map/convert_element_type | solution.py:34
  35.7 192.7 %all_to_all.15 = bf16[2,16,128,1024]{3,2,0,1:T(8,128)(2,1)} all-to-all(bf16[2,16,128,1024]{3,2,0,1:T(8,128)(2,1)} %copy.26), channel_id=1, replica_groups=mesh['groups'=2,'chan'=4,'tm'=4] {'chan'}, dimensions={1} | all-to-all | bytes 16777216 | tf_op jit(solution)/shard_map/all_to_all | solution.py:35
  228.3 8.4 %copy.52 = bf16[2,4,4,128,1024]{4,3,1,2,0:T(8,128)(2,1)} copy(bf16[2,4,4,128,1024]{4,3,0,2,1:T(8,128)(2,1)} %bitcast.115) | data formatting | bytes 16777216 | tf_op jit(solution)/shard_map/all_to_all | solution.py:35
  236.7 6.1 fusion.172
  242.8 17.7 %fusion.10 = f32[4,1024,1024]{2,1,0:T(8,128)} fusion(bf16[4,512,1024]{2,1,0:T(8,128)(2,1)} %bitcast.118, bf16[4,512,1024]{2,1,0:T(8,128)(2,1)} %bitcast.116), kind=kOutput, calls=%fused_computation.13 | convolution fusion | flops 8606711808 | bytes 25165824 | tf_op jit(solution)/shard_map/cat,cbt->cab/dot_general | solution.py:22
  260.4 8.8 %fusion.12 = (bf16[4,512,512]{2,1,0:T(8,128)(2,1)}, bf16[4,512,512]{2,1,0:T(8,128)(2,1)}) fusion(f32[4,1024,1024]{2,1,0:T(8,128)} %fusion.10), kind=kLoop, calls=%fused_computation.17 | loop fusion | flops 4194304 | bytes 20971520 | tf_op jit(solution)/shard_map/convert_element_type | solution.py:43
  269.3 0.6 copy-done.6
  269.9 3.4 gather_fusion
  273.3 80.9 %all-reduce.3.cloned.1.call-done = (bf16[4,512,512]{2,1,0:T(8,128)(2,1)}, bf16[4,512,512]{2,1,0:T(8,128)(2,1)}) async-done(((bf16[4,512,512]{2,1,0:T(8,128)(2,1)}, bf16[4,512,512]{2,1,0:T(8,128)(2,1)}), (bf16[4,512,512]{2,1,0:T(8,128)(2,1)}, bf16[4,512,512]{2,1,0:T(8,128)(2,1)})) %all-reduce.3.cloned.1.call-update) | async-done | bytes 4194320 | tf_op jit(solution)/shard_map/psum | solution.py:44
  354.2 6.3 convert_multiply_fusion.15
  360.4 60.3 %copy.28 = f32[4,512,512]{0,2,1:T(8,128)} copy(f32[4,512,512]{2,1,0:T(8,128)} %get-tuple-element.27) | data formatting | bytes 8388608 | tf_op jit(solution)/shard_map/div | solution.py:46
  420.8 5.7 gather_fusion.1
  426.7 8.6 %fusion.26 = f32[4,512,128]{2,1,0:T(8,128)S(1)} fusion(bf16[4,512,512]{2,1,0:T(8,128)(2,1)S(1)} %copy-done.2, f32[512,4,128]{2,0,1:T(8,128)} %gather_fusion, f32[4]{0:T(128)S(1)} %get-tuple-element.16, pred[512]{0:T(512)(128)(4,1)S(1)} %compare_and_fusion), kind=kOutput, calls=%fused_computation.35 | convolution fusion | flops 1613234176 | bytes 4194832 | tf_op jit(solution)/shard_map/cjk,ckb->cjb/dot_general | solution.py:66
  435.4 9.0 %fusion.25 = f32[4,512,128]{2,1,0:T(8,128)S(1)} fusion(bf16[4,512,512]{2,1,0:T(8,128)(2,1)S(1)} %copy-done.2, f32[512,4,128]{2,0,1:T(8,128)} %gather_fusion, f32[4]{0:T(128)S(1)} %get-tuple-element.16, pred[512]{0:T(512)(128)(4,1)S(1)} %compare_and_fusion), kind=kOutput, calls=%fused_computation.34 | convolution fusion | flops 1613234176 | bytes 4194832 | tf_op jit(solution)/shard_map/cjk,ckb->cjb/dot_general | solution.py:69
  444.4 11.0 %fusion.112 = f32[4,512,128]{2,1,0:T(8,128)S(1)} fusion(f32[4,512,128]{2,1,0:T(8,128)S(1)} %fusion.26, bf16[4,512,512]{2,1,0:T(8,128)(2,1)S(1)} %copy-done.3, f32[512,4,128]{2,0,1:T(8,128)S(1)} %copy-done.5, f32[4]{0:T(128)S(1)} %get-tuple-element.48, pred[512]{0:T(512)(128)(4,1)S(1)} %compare_and_fusion, f32[4]{0:T(128)S(1)} %get-tuple-element.16), kind=kOutput, calls=%fused_computation.124 | convolution fusion | flops 1614807040 | bytes 5243424 | tf_op jit(solution)/shard_map/cjk,ckb->cjb/dot_general | solution.py:66
  455.3 10.7 %fusion.108 = f32[4,512,128]{2,1,0:T(8,128)S(1)} fusion(f32[4,512,128]{2,1,0:T(8,128)S(1)} %fusion.25, bf16[4,512,512]{2,1,0:T(8,128)(2,1)S(1)} %copy-done.3, f32[512,4,128]{2,0,1:T(8,128)S(1)} %copy-done.5, f32[4]{0:T(128)S(1)} %get-tuple-element.48, pred[512]{0:T(512)(128)(4,1)S(1)} %compare_and_fusion, f32[4]{0:T(128)S(1)} %get-tuple-element.16), kind=kOutput, calls=%fused_computation.120 | convolution fusion | flops 1614807040 | bytes 5243424 | tf_op jit(solution)/shard_map/cjk,ckb->cjb/dot_general | solution.py:69
  466.1 7.5 %fusion.23 = f32[4,512,128]{2,1,0:T(8,128)S(1)} fusion(bf16[4,512,512]{2,1,0:T(8,128)(2,1)S(1)} %copy-done.2, f32[4,512,128]{2,1,0:T(8,128)S(1)} %fusion.112, f32[4]{0:T(128)S(1)} %get-tuple-element.46, f32[4]{0:T(128)S(1)} %get-tuple-element.47, f32[512,4,128]{2,0,1:T(8,128)S(1)} %copy-done.5, f32[4]{0:T(128)S(1)} %get-tuple-element.16, ...), kind=kOutput, calls=%fused_computation.32 | convolution fusion | flops 1614020608 | bytes 5243440 | tf_op jit(solution)/shard_map/cjk,ckb->cjb/dot_general | solution.py:69
  473.6 7.7 %fusion.24 = f32[4,512,128]{2,1,0:T(8,128)S(1)} fusion(bf16[4,512,512]{2,1,0:T(8,128)(2,1)S(1)} %copy-done.2, f32[4,512,128]{2,1,0:T(8,128)S(1)} %fusion.108, f32[4]{0:T(128)S(1)} %get-tuple-element.46, f32[4]{0:T(128)S(1)} %get-tuple-element.47, f32[512,4,128]{2,0,1:T(8,128)S(1)} %copy-done.5, f32[4]{0:T(128)S(1)} %get-tuple-element.16, ...), kind=kOutput, calls=%fused_computation.33 | convolution fusion | flops 1614020608 | bytes 5243440 | tf_op jit(solution)/shard_map/cjk,ckb->cjb/dot_general | solution.py:66
  481.4 11.3 %fusion.110 = f32[4,512,128]{2,1,0:T(8,128)S(1)} fusion(f32[4,512,128]{2,1,0:T(8,128)S(1)} %fusion.112, f32[4,512,128]{2,1,0:T(8,128)S(1)} %fusion.24, bf16[4,512,512]{2,1,0:T(8,128)(2,1)S(1)} %copy-done.3, f32[4]{0:T(128)S(1)} %get-tuple-element.48, f32[4]{0:T(128)S(1)} %get-tuple-element.46, f32[4]{0:T(128)S(1)} %get-tuple-element.47, ...), kind=kOutput, calls=%fused_computation.122 | convolution fusion | flops 1616379904 | bytes 6292032 | tf_op jit(solution)/shard_map/cjk,ckb->cjb/dot_general | solution.py:66
  492.7 11.8 %multiply_add_fusion.10 = (f32[4,512,128]{2,1,0:T(8,128)S(1)}, f32[4,512,128]{2,1,0:T(8,128)S(1)}, f32[4,512,128]{2,1,0:T(8,128)S(1)}) fusion(f32[4]{0:T(128)S(1)} %get-tuple-element.44, f32[4]{0:T(128)S(1)} %get-tuple-element.45, f32[4,512,128]{2,1,0:T(8,128)S(1)} %fusion.108, f32[4]{0:T(128)S(1)} %get-tuple-element.46, f32[4]{0:T(128)S(1)} %get-tuple-element.47, ...), kind=kOutput, calls=%fused_computation.146 | convolution fusion | flops 1619001344 | bytes 10486368 | tf_op jit(solution)/shard_map/cjk,ckb->cjb/dot_general | solution.py:69
  504.5 3.9 fusion.22
  508.5 3.9 fusion.21
  512.4 4.2 fusion.106
  516.7 4.1 fusion.100
  520.7 4.1 fusion.19
  524.8 4.1 fusion.20
  528.9 4.7 fusion.102
  533.6 4.5 multiply_add_fusion.6
  538.0 3.9 fusion.17
  542.0 4.1 fusion.18
  546.1 4.0 fusion.98
  550.2 4.0 fusion.92
  554.2 4.3 fusion.16
  558.5 4.1 fusion.15
  562.6 4.2 fusion.94
  566.8 4.6 fusion.87
  571.4 4.2 fusion.13
  575.6 4.2 fusion.14
  579.8 8.4 %fusion.114 = f32[4,512,128]{2,1,0:T(8,128)S(1)} fusion(f32[4,512,128]{2,1,0:T(8,128)S(1)} %fusion.94, f32[4,512,128]{2,1,0:T(8,128)S(1)} %fusion.14, bf16[4,512,512]{2,1,0:T(8,128)(2,1)S(1)} %copy-done.3, f32[4,512,128]{2,1,0:T(8,128)S(1)} %get-tuple-element.34, f32[4,512,128]{2,1,0:T(8,128)S(1)} %get-tuple-element.30, f32[4]{0:T(128)S(1)} %get-tuple-element.35, ...), kind=kOutput, calls=%fused_computation.126 | convolution fusion | flops 1621622784 | bytes 11535040 | tf_op jit(solution)/shard_map/cjk,ckb->cjb/dot_general | solution.py:66
  588.2 9.0 %fusion.118 = (f32[4,128]{1,0:T(4,128)S(1)}, f32[4,512,128]{2,1,0:T(8,128)S(1)}) fusion(f32[4,512,128]{2,1,0:T(8,128)S(1)} %fusion.114, f32[512,4,128]{2,0,1:T(8,128)S(1)} %copy-done.5, pred[512]{0:T(512)(128)(4,1)S(1)} %compare_and_fusion, f32[4,512,128]{2,1,0:T(8,128)S(1)} %fusion.87, f32[4]{0:T(128)S(1)} %get-tuple-element.48, ...), kind=kOutput, calls=%fused_computation.133 | convolution fusion | flops 1622670848 | bytes 12585664 | tf_op jit(solution)/shard_map/cjk,ckb->cjb/dot_general | solution.py:69
  597.5 1.1 pad_maximum_fusion.4
  598.5 35.3 %all-gather.2.cloned.1.call-done = bf16[4,2,512,512]{3,2,0,1:T(8,128)(2,1)} async-done(((bf16[4,2,512,128]{3,2,0,1:T(8,128)(2,1)}), bf16[4,2,512,512]{3,2,0,1:T(8,128)(2,1)}) %all-gather.2.cloned.1.call-update) | async-done | bytes 4194320 | tf_op jit(solution)/shard_map/all_gather | solution.py:85
  633.9 2.7 slice_bitcast_fusion
  636.5 0.8 copy-done.4
  637.4 2.3 maximum_bitcast_fusion
  639.8 14.0 %fusion.5 = bf16[4,1024,2,512]{3,1,2,0:T(8,128)(2,1)} fusion(bf16[4,512,1024]{2,1,0:T(8,128)(2,1)} %bitcast.119, bf16[4,512,1024]{2,1,0:T(8,128)(2,1)} %bitcast.117, bf16[4,1024,1,512]{3,1,0,2:T(8,128)(2,1)} %get-tuple-element.26, bf16[4,1024,1,512]{3,1,0,2:T(8,128)(2,1)S(1)} %get-tuple-element.25), kind=kOutput, calls=%fused_computation.12 | convolution fusion | flops 8615100416 | bytes 25165824 | tf_op jit(solution)/shard_map/cat,cakb->ctkb/dot_general | solution.py:95
  653.7 16.5 %copy.31 = bf16[4,1024,2,512]{3,2,1,0:T(2,128)(2,1)} copy(bf16[4,1024,2,512]{3,1,2,0:T(8,128)(2,1)} %fusion.5) | data formatting | bytes 16777216 | tf_op jit(solution)/shard_map/convert_element_type | solution.py:96
  (30 shorter events, 1.0 us)
Async XLA Ops:
  6.5 263.4 %copy-start = (f32[4,512,128]{2,1,0:T(8,128)S(1)}, f32[4,512,128]{2,1,0:T(8,128)}, u32[]{:S(2)}) copy-start(f32[4,512,128]{2,1,0:T(8,128)} %param.7) | copy-start | bytes 3145732
  6.5 347.6 %all-reduce.3.cloned.1.call-start = ((), (), s32[]{:S(2)}) async-start(), calls=%async_computation.2 | async-start | bytes 8388608 | tf_op jit(solution)/shard_map/psum | solution.py:44
  269.2 0.7 copy-start.6
  269.3 364.6 %all-gather.2.cloned.1.call-start = ((), (), s32[]{:S(2)}) async-start(), calls=%async_computation.1 | async-start | bytes 5242880 | tf_op jit(solution)/shard_map/all_gather | solution.py:85
  360.4 66.3 %copy-start.2 = (bf16[4,512,512]{2,1,0:T(8,128)(2,1)S(1)}, bf16[4,512,512]{2,1,0:T(8,128)(2,1)}, u32[]{:S(2)}) copy-start(bf16[4,512,512]{2,1,0:T(8,128)(2,1)} %get-tuple-element.5) | copy-start | bytes 6291460
  435.4 9.0 %copy-start.3 = (bf16[4,512,512]{2,1,0:T(8,128)(2,1)S(1)}, bf16[4,512,512]{2,1,0:T(8,128)(2,1)}, u32[]{:S(2)}) copy-start(bf16[4,512,512]{2,1,0:T(8,128)(2,1)} %get-tuple-element.6) | copy-start | bytes 6291460
  435.4 9.0 %copy-start.5 = (f32[512,4,128]{2,0,1:T(8,128)S(1)}, f32[512,4,128]{2,0,1:T(8,128)}, u32[]{:S(2)}) copy-start(f32[512,4,128]{2,0,1:T(8,128)} %gather_fusion) | copy-start | bytes 3145732
  633.9 3.4 copy-start.4
  653.7 16.5 %copy-start.1 = (f32[4,512,128]{2,1,0:T(8,128)S(1)}, f32[4,512,128]{2,1,0:T(8,128)}, u32[]{:S(2)}) copy-start(f32[4,512,128]{2,1,0:T(8,128)} %param.7) | copy-start | bytes 3145732
Sparse Core Ops, SparseCore 0:
  269.4 84.7 all-reduce.2
  598.7 35.1 all-gather.1
where the time goes:
time: 687 us; the launch traced here: 677 us
  matrix products  219 us (32%)
  blocking collectives  193 us (28%)
  local copies, waits for them, and re-layouts  116 us (17%)
  waiting for transfers between devices  116 us (17%)
  other arithmetic  19.3 us (3%)
  between operations  13.9 us (2%)
    all_to_all x1, blocking collectives, local(): lax.all_to_all(spectra, 'chan', split_axis=1, concat_axis=2, tiled=True)  193 us
    psum x1, waiting for transfers between devices, local(): lax.psum(part_imag.astype(jnp.bfloat16), 'tm').astype(jnp.float32)  80.9 us
    div x1, local copies, waits for them, and re-layouts, local(): cov_real = cov_real / spectra_total  60.3 us
    dot_general x7, matrix products, local(): jnp.einsum('cjk,ckb->cjb', cov_real, dir_imag, precision=high)  48.6 us
    dot_general x7, matrix products, local(): jnp.einsum('cjk,ckb->cjb', cov_real, dir_real, precision=high)  47.8 us
    dot_general x7, matrix products, local(): jnp.einsum('cjk,ckb->cjb', cov_imag, dir_imag, precision=high)  37.1 us
    dot_general x7, matrix products, local(): jnp.einsum('cjk,ckb->cjb', cov_imag, dir_real, precision=high)  36.7 us
    all_gather x1, waiting for transfers between devices, local(): block_part = lax.all_gather(weights, 'tm', axis=3, tiled=True)  35.3 us
  transfers between devices with their start and end apart: 2, of which 2 were waited for; matrix products, arithmetic and copies ran while one was open for 1% of the time, Pallas kernels for 0%

commit v1 on v0

--- a/solution.py
+++ b/solution.py
@@ -41,7 +41,7 @@
     part_imag = gram_sum[:, stations:, :stations] - gram_sum[:, :stations, stations:]
     cov_real, cov_imag = (
         lax.psum(part_real.astype(jnp.bfloat16), "tm").astype(jnp.float32),
-        lax.psum(part_imag.astype(jnp.bfloat16), "tm").astype(jnp.float32),
+        jnp.sum(lax.all_gather(part_imag.astype(jnp.bfloat16), "tm"), axis=0).astype(jnp.float32),
     )
     cov_real = cov_real / spectra_total
     cov_imag = cov_imag / spectra_total

time: 687 us -> 714 us (1.039)
  waiting for transfers between devices: 116 us -> 138 us
    all_gather x0 -> x1, waiting for transfers between devices: none -> 53.3 us  [local(): lax.all_gather(part_imag.astype(jnp.bfloat16), 'tm')]
    psum x1, waiting for transfers between devices: 80.9 us -> 48.7 us  [local(): lax.psum(part_real.astype(jnp.bfloat16), 'tm').astype(jnp.float32)]
  transfers between devices with their start and end apart: 2 -> 3, of which waited for: 2 -> 3; matrix products, arithmetic and copies ran while one was open for 1% -> 1% of each run, Pallas kernels for 0% -> 0%
where the time goes in v1:
time: 714 us; the launch traced here: 704 us
  matrix products  219 us (31%)
  blocking collectives  192 us (27%)
  waiting for transfers between devices  138 us (19%)
  local copies, waits for them, and re-layouts  117 us (16%)
  other arithmetic  23.7 us (3%)
  between operations  13.6 us (2%)
    all_to_all x1, blocking collectives, local(): lax.all_to_all(spectra, 'chan', split_axis=1, concat_axis=2, tiled=True)  192 us
    div x1, local copies, waits for them, and re-layouts, local(): cov_real = cov_real / spectra_total  61.6 us
    all_gather x1, waiting for transfers between devices, local(): lax.all_gather(part_imag.astype(jnp.bfloat16), 'tm')  53.3 us
    psum x1, waiting for transfers between devices, local(): lax.psum(part_real.astype(jnp.bfloat16), 'tm').astype(jnp.float32)  48.7 us
    dot_general x7, matrix products, local(): jnp.einsum('cjk,ckb->cjb', cov_real, dir_imag, precision=high)  48.5 us
    dot_general x7, matrix products, local(): jnp.einsum('cjk,ckb->cjb', cov_real, dir_real, precision=high)  47.6 us
    dot_general x7, matrix products, local(): jnp.einsum('cjk,ckb->cjb', cov_imag, dir_imag, precision=high)  37 us
    dot_general x7, matrix products, local(): jnp.einsum('cjk,ckb->cjb', cov_imag, dir_real, precision=high)  36.9 us
  transfers between devices with their start and end apart: 3, of which 3 were waited for; matrix products, arithmetic and copies ran while one was open for 1% of the time, Pallas kernels for 0%

profile of v1, /device:TPU:0, one launch (start us, length us, event | category | flops | bytes accessed | tf_op | source)
XLA Modules:
  0.0 703.6 jit_solution(1021359503151748612)
XLA Ops:
  6.7 17.6 %multiply_convert_fusion = bf16[2,16,128,1024]{3,1,2,0:T(8,128)(2,1)} fusion(f32[128]{0:T(128)} %param.5, bf16[2,16,32,1]{2,1,3,0:T(8,128)(2,1)S(1)} %bitcast.122, bf16[4,8,128,1024]{3,2,1,0:T(8,128)(2,1)} %bitcast.123), kind=kOutput, calls=%fused_computation.2 | convolution fusion | flops 276824064 | bytes 16779776 | tf_op jit(solution)/shard_map/dot_general | solution.py:30
  24.4 11.3 %copy.26 = bf16[2,16,128,1024]{3,2,0,1:T(8,128)(2,1)} copy(bf16[2,16,128,1024]{3,1,2,0:T(8,128)(2,1)} %multiply_convert_fusion) | data formatting | bytes 16777216 | tf_op jit(solution)/shard_map/convert_element_type | solution.py:34
  35.7 192.4 %all_to_all.15 = bf16[2,16,128,1024]{3,2,0,1:T(8,128)(2,1)} all-to-all(bf16[2,16,128,1024]{3,2,0,1:T(8,128)(2,1)} %copy.26), channel_id=1, replica_groups=mesh['groups'=2,'chan'=4,'tm'=4] {'chan'}, dimensions={1} | all-to-all | bytes 16777216 | tf_op jit(solution)/shard_map/all_to_all | solution.py:35
  228.0 8.4 %copy.52 = bf16[2,4,4,128,1024]{4,3,1,2,0:T(8,128)(2,1)} copy(bf16[2,4,4,128,1024]{4,3,0,2,1:T(8,128)(2,1)} %bitcast.116) | data formatting | bytes 16777216 | tf_op jit(solution)/shard_map/all_to_all | solution.py:35
  236.4 6.1 fusion.172
  242.5 17.6 %fusion.10 = f32[4,1024,1024]{2,1,0:T(8,128)} fusion(bf16[4,512,1024]{2,1,0:T(8,128)(2,1)} %bitcast.120, bf16[4,512,1024]{2,1,0:T(8,128)(2,1)} %bitcast.118), kind=kOutput, calls=%fused_computation.13 | convolution fusion | flops 8606711808 | bytes 25165824 | tf_op jit(solution)/shard_map/cat,cbt->cab/dot_general | solution.py:22
  260.1 8.8 %fusion.12 = (bf16[4,512,512]{2,1,0:T(8,128)(2,1)}, bf16[4,512,512]{2,1,0:T(8,128)(2,1)}) fusion(f32[4,1024,1024]{2,1,0:T(8,128)} %fusion.10), kind=kLoop, calls=%fused_computation.17 | loop fusion | flops 4194304 | bytes 20971520 | tf_op jit(solution)/shard_map/convert_element_type | solution.py:43
  269.7 3.4 gather_fusion
  273.1 53.3 %all-gather.6.cloned.1.call-done = bf16[16,512,512]{2,1,0:T(8,128)(2,1)} async-done(((bf16[4,512,512]{2,1,0:T(8,128)(2,1)}), bf16[16,512,512]{2,1,0:T(8,128)(2,1)}) %all-gather.6.cloned.1.call-update) | async-done | bytes 8388624 | tf_op jit(solution)/shard_map/all_gather | solution.py:44
  326.5 5.1 reduce_sum.40
  331.5 48.7 %all-reduce.2.cloned.1.call-done = bf16[4,512,512]{2,1,0:T(8,128)(2,1)} async-done(((bf16[4,512,512]{2,1,0:T(8,128)(2,1)}), bf16[4,512,512]{2,1,0:T(8,128)(2,1)}) %all-reduce.2.cloned.1.call-update) | async-done | bytes 2097168 | tf_op jit(solution)/shard_map/psum | solution.py:43
  380.2 5.6 convert_multiply_fusion.15
  385.9 61.6 %copy.28 = f32[4,512,512]{0,2,1:T(8,128)} copy(f32[4,512,512]{2,1,0:T(8,128)} %get-tuple-element.25) | data formatting | bytes 8388608 | tf_op jit(solution)/shard_map/div | solution.py:46
  447.5 5.9 gather_fusion.1
  453.7 8.7 %fusion.26 = f32[4,512,128]{2,1,0:T(8,128)S(1)} fusion(bf16[4,512,512]{2,1,0:T(8,128)(2,1)S(1)} %reduce_sum.40, f32[512,4,128]{2,0,1:T(8,128)} %gather_fusion, f32[4]{0:T(128)S(1)} %get-tuple-element.14, pred[512]{0:T(512)(128)(4,1)S(1)} %compare_and_fusion), kind=kOutput, calls=%fused_computation.35 | convolution fusion | flops 1613234176 | bytes 4194832 | tf_op jit(solution)/shard_map/cjk,ckb->cjb/dot_general | solution.py:66
  462.3 8.9 %fusion.25 = f32[4,512,128]{2,1,0:T(8,128)S(1)} fusion(bf16[4,512,512]{2,1,0:T(8,128)(2,1)S(1)} %reduce_sum.40, f32[512,4,128]{2,0,1:T(8,128)} %gather_fusion, f32[4]{0:T(128)S(1)} %get-tuple-element.14, pred[512]{0:T(512)(128)(4,1)S(1)} %compare_and_fusion), kind=kOutput, calls=%fused_computation.34 | convolution fusion | flops 1613234176 | bytes 4194832 | tf_op jit(solution)/shard_map/cjk,ckb->cjb/dot_general | solution.py:69
  471.3 10.8 %fusion.112 = f32[4,512,128]{2,1,0:T(8,128)S(1)} fusion(f32[4,512,128]{2,1,0:T(8,128)S(1)} %fusion.26, bf16[4,512,512]{2,1,0:T(8,128)(2,1)S(1)} %copy-done.2, f32[512,4,128]{2,0,1:T(8,128)S(1)} %copy-done.4, f32[4]{0:T(128)S(1)} %get-tuple-element.46, pred[512]{0:T(512)(128)(4,1)S(1)} %compare_and_fusion, f32[4]{0:T(128)S(1)} %get-tuple-element.14), kind=kOutput, calls=%fused_computation.124 | convolution fusion | flops 1614807040 | bytes 5243424 | tf_op jit(solution)/shard_map/cjk,ckb->cjb/dot_general | solution.py:66
  482.1 7.5 %fusion.23 = f32[4,512,128]{2,1,0:T(8,128)S(1)} fusion(bf16[4,512,512]{2,1,0:T(8,128)(2,1)S(1)} %reduce_sum.40, f32[4,512,128]{2,1,0:T(8,128)S(1)} %fusion.112, f32[4]{0:T(128)S(1)} %get-tuple-element.44, f32[4]{0:T(128)S(1)} %get-tuple-element.45, f32[512,4,128]{2,0,1:T(8,128)S(1)} %copy-done.4, f32[4]{0:T(128)S(1)} %get-tuple-element.14, ...), kind=kOutput, calls=%fused_computation.32 | convolution fusion | flops 1614020608 | bytes 5243440 | tf_op jit(solution)/shard_map/cjk,ckb->cjb/dot_general | solution.py:69
  489.6 11.0 %fusion.108 = f32[4,512,128]{2,1,0:T(8,128)S(1)} fusion(f32[4,512,128]{2,1,0:T(8,128)S(1)} %fusion.25, bf16[4,512,512]{2,1,0:T(8,128)(2,1)S(1)} %copy-done.2, f32[512,4,128]{2,0,1:T(8,128)S(1)} %copy-done.4, f32[4]{0:T(128)S(1)} %get-tuple-element.46, pred[512]{0:T(512)(128)(4,1)S(1)} %compare_and_fusion, f32[4]{0:T(128)S(1)} %get-tuple-element.14), kind=kOutput, calls=%fused_computation.120 | convolution fusion | flops 1614807040 | bytes 5243424 | tf_op jit(solution)/shard_map/cjk,ckb->cjb/dot_general | solution.py:69
  500.6 7.7 %fusion.24 = f32[4,512,128]{2,1,0:T(8,128)S(1)} fusion(bf16[4,512,512]{2,1,0:T(8,128)(2,1)S(1)} %reduce_sum.40, f32[4,512,128]{2,1,0:T(8,128)S(1)} %fusion.108, f32[4]{0:T(128)S(1)} %get-tuple-element.44, f32[4]{0:T(128)S(1)} %get-tuple-element.45, f32[512,4,128]{2,0,1:T(8,128)S(1)} %copy-done.4, f32[4]{0:T(128)S(1)} %get-tuple-element.14, ...), kind=kOutput, calls=%fused_computation.33 | convolution fusion | flops 1614020608 | bytes 5243440 | tf_op jit(solution)/shard_map/cjk,ckb->cjb/dot_general | solution.py:66
  508.3 11.1 %fusion.110 = f32[4,512,128]{2,1,0:T(8,128)S(1)} fusion(f32[4,512,128]{2,1,0:T(8,128)S(1)} %fusion.112, f32[4,512,128]{2,1,0:T(8,128)S(1)} %fusion.24, bf16[4,512,512]{2,1,0:T(8,128)(2,1)S(1)} %copy-done.2, f32[4]{0:T(128)S(1)} %get-tuple-element.46, f32[4]{0:T(128)S(1)} %get-tuple-element.44, f32[4]{0:T(128)S(1)} %get-tuple-element.45, ...), kind=kOutput, calls=%fused_computation.122 | convolution fusion | flops 1616379904 | bytes 6292032 | tf_op jit(solution)/shard_map/cjk,ckb->cjb/dot_general | solution.py:66
  519.4 12.1 %multiply_add_fusion.10 = (f32[4,512,128]{2,1,0:T(8,128)S(1)}, f32[4,512,128]{2,1,0:T(8,128)S(1)}, f32[4,512,128]{2,1,0:T(8,128)S(1)}) fusion(f32[4]{0:T(128)S(1)} %get-tuple-element.42, f32[4]{0:T(128)S(1)} %get-tuple-element.43, f32[4,512,128]{2,1,0:T(8,128)S(1)} %fusion.108, f32[4]{0:T(128)S(1)} %get-tuple-element.44, f32[4]{0:T(128)S(1)} %get-tuple-element.45, ...), kind=kOutput, calls=%fused_computation.146 | convolution fusion | flops 1619001344 | bytes 10486368 | tf_op jit(solution)/shard_map/cjk,ckb->cjb/dot_general | solution.py:69
  531.5 3.9 fusion.22
  535.4 3.9 fusion.21
  539.3 4.2 fusion.106
  543.5 4.1 fusion.19
  547.6 4.0 fusion.100
  551.6 4.1 fusion.20
  555.7 4.4 fusion.102
  560.2 4.5 multiply_add_fusion.6
  564.7 3.9 fusion.17
  568.6 4.3 fusion.18
  573.0 4.0 fusion.92
  576.9 4.1 fusion.16
  581.0 4.2 fusion.98
  585.3 4.1 fusion.15
  589.4 4.3 fusion.94
  593.6 4.4 fusion.13
  598.1 4.1 fusion.87
  602.2 4.2 fusion.14
  606.4 8.6 %fusion.114 = f32[4,512,128]{2,1,0:T(8,128)S(1)} fusion(f32[4,512,128]{2,1,0:T(8,128)S(1)} %fusion.94, f32[4,512,128]{2,1,0:T(8,128)S(1)} %fusion.14, bf16[4,512,512]{2,1,0:T(8,128)(2,1)S(1)} %copy-done.2, f32[4,512,128]{2,1,0:T(8,128)S(1)} %get-tuple-element.32, f32[4,512,128]{2,1,0:T(8,128)S(1)} %get-tuple-element.28, f32[4]{0:T(128)S(1)} %get-tuple-element.33, ...), kind=kOutput, calls=%fused_computation.126 | convolution fusion | flops 1621622784 | bytes 11535040 | tf_op jit(solution)/shard_map/cjk,ckb->cjb/dot_general | solution.py:66
  615.0 8.9 %fusion.118 = (f32[4,128]{1,0:T(4,128)S(1)}, f32[4,512,128]{2,1,0:T(8,128)S(1)}) fusion(f32[4,512,128]{2,1,0:T(8,128)S(1)} %fusion.114, f32[512,4,128]{2,0,1:T(8,128)S(1)} %copy-done.4, pred[512]{0:T(512)(128)(4,1)S(1)} %compare_and_fusion, f32[4,512,128]{2,1,0:T(8,128)S(1)} %fusion.87, f32[4]{0:T(128)S(1)} %get-tuple-element.46, ...), kind=kOutput, calls=%fused_computation.133 | convolution fusion | flops 1622670848 | bytes 12585664 | tf_op jit(solution)/shard_map/cjk,ckb->cjb/dot_general | solution.py:69
  624.1 1.1 pad_maximum_fusion.4
  625.2 35.3 %all-gather.4.cloned.1.call-done = bf16[4,2,512,512]{3,2,0,1:T(8,128)(2,1)} async-done(((bf16[4,2,512,128]{3,2,0,1:T(8,128)(2,1)}), bf16[4,2,512,512]{3,2,0,1:T(8,128)(2,1)}) %all-gather.4.cloned.1.call-update) | async-done | bytes 4194320 | tf_op jit(solution)/shard_map/all_gather | solution.py:85
  660.5 2.7 slice_bitcast_fusion
  664.1 2.3 maximum_bitcast_fusion
  666.4 14.0 %fusion.5 = bf16[4,1024,2,512]{3,1,2,0:T(8,128)(2,1)} fusion(bf16[4,512,1024]{2,1,0:T(8,128)(2,1)} %bitcast.121, bf16[4,512,1024]{2,1,0:T(8,128)(2,1)} %bitcast.119, bf16[4,1024,1,512]{3,1,0,2:T(8,128)(2,1)} %get-tuple-element.24, bf16[4,1024,1,512]{3,1,0,2:T(8,128)(2,1)S(1)} %get-tuple-element.23), kind=kOutput, calls=%fused_computation.12 | convolution fusion | flops 8615100416 | bytes 25165824 | tf_op jit(solution)/shard_map/cat,cakb->ctkb/dot_general | solution.py:95
  680.3 16.5 %copy.31 = bf16[4,1024,2,512]{3,2,1,0:T(2,128)(2,1)} copy(bf16[4,1024,2,512]{3,1,2,0:T(8,128)(2,1)} %fusion.5) | data formatting | bytes 16777216 | tf_op jit(solution)/shard_map/convert_element_type | solution.py:96
  (32 shorter events, 2.5 us)
Async XLA Ops:
  6.5 263.2 %copy-start = (f32[4,512,128]{2,1,0:T(8,128)S(1)}, f32[4,512,128]{2,1,0:T(8,128)}, u32[]{:S(2)}) copy-start(f32[4,512,128]{2,1,0:T(8,128)} %param.7) | copy-start | bytes 3145732
  6.5 319.9 %all-gather.6.cloned.1.call-start = ((), (), s32[]{:S(2)}) async-start(), calls=%async_computation.3 | async-start | bytes 10485760 | tf_op jit(solution)/shard_map/all_gather | solution.py:44
  268.9 0.8 copy-start.5
  268.9 111.3 %all-reduce.2.cloned.1.call-start = ((), (), s32[]{:S(2)}) async-start(), calls=%async_computation.1 | async-start | bytes 4194304 | tf_op jit(solution)/shard_map/psum | solution.py:43
  269.7 390.8 %all-gather.4.cloned.1.call-start = ((), (), s32[]{:S(2)}) async-start(), calls=%async_computation.2 | async-start | bytes 5242880 | tf_op jit(solution)/shard_map/all_gather | solution.py:85
  462.3 9.0 %copy-start.2 = (bf16[4,512,512]{2,1,0:T(8,128)(2,1)S(1)}, bf16[4,512,512]{2,1,0:T(8,128)(2,1)}, u32[]{:S(2)}) copy-start(bf16[4,512,512]{2,1,0:T(8,128)(2,1)} %all-reduce.2.cloned.1.call-done) | copy-start | bytes 6291460
  462.3 9.0 %copy-start.4 = (f32[512,4,128]{2,0,1:T(8,128)S(1)}, f32[512,4,128]{2,0,1:T(8,128)}, u32[]{:S(2)}) copy-start(f32[512,4,128]{2,0,1:T(8,128)} %gather_fusion) | copy-start | bytes 3145732
  660.5 3.4 copy-start.3
  680.3 16.5 %copy-start.1 = (f32[4,512,128]{2,1,0:T(8,128)S(1)}, f32[4,512,128]{2,1,0:T(8,128)}, u32[]{:S(2)}) copy-start(f32[4,512,128]{2,1,0:T(8,128)} %param.7) | copy-start | bytes 3145732
Sparse Core Ops, SparseCore 0:
  269.0 57.3 all-gather.5
  328.8 51.3 all-reduce.1
  625.3 35.0 all-gather.3
